TPU v7x, 512 devices: a whole 4x8x8 slice. The times are simulated.
512 devices in a mesh: clus: 256 (over z, y, x), samp: 2 (over core).
Axes of the slice: x: 4, y: 8, z: 8, core: 2. Of those that a mesh axis runs over, the one named last changes fastest.
Arguments:
- samples: float32 [262144, 256], P('clus', 'samp'), may hold values from -8 to 8
- sketch: float32 [256, 128], P('samp'), may hold values from -0.375 to 0.375
- leaf_slot: int32 [256, 4], P('clus'), may hold values from 0 to 3, each once within a row
Outputs:
- leaf_basis: float32 [262144, 128], P('clus')
- local_transfer: float32 [768, 256, 128], P('clus')
- top_transfer: float32 [256, 256, 128], P('clus')
- root_factor: float32 [128, 128], replicated
Inputs may be any that keep to these rules, and one draw needn't show every extreme that they name: Each row of leaf_slot names every number from 0 to 3 once.
All inputs are finite; a program needn't handle non-finite values.
Results may differ from a plain program's by a relative error of at most 0.0003.
Values sent between devices are 32-bit elements; how exact they have to be, the bound alone decides.
No kernel may reach another device: no remote copies, remote signals or barrier semaphores. Data moves between devices by JAX's collectives and lax.ppermute only.
A program may use at most 64 MiB of HBM per device.

v0:
```python
import jax
import jax.numpy as jnp
from jax import lax
from jax.sharding import PartitionSpec as P

NS_STEPS = 5
highest = lax.Precision.HIGHEST


def from_partner(block, axis, apart):
    count = lax.axis_size(axis)
    route = []
    for low in range(count):
        high = low | 1 << apart
        if high != low and high < count:
            route += [(low, high), (high, low)]
    return lax.ppermute(block, axis, route)


def factor(stacked):
    gram_matrix = jnp.einsum("mrk,mrl->mkl", stacked, stacked, precision=highest)
    width = gram_matrix.shape[1]
    identity = jnp.eye(width, dtype=jnp.float32)
    scale = jnp.einsum("mkk->m", gram_matrix)[:, None, None] + 1e-06
    start_root = gram_matrix / scale
    start_inverse = jnp.broadcast_to(identity, gram_matrix.shape)

    def newton_step(index, carry):
        root, inverse = carry
        middle = 1.5 * identity - 0.5 * jnp.einsum("mkl,mlj->mkj", inverse, root, precision=highest)
        return (
            jnp.einsum("mkl,mlj->mkj", root, middle, precision=highest),
            jnp.einsum("mkl,mlj->mkj", middle, inverse, precision=highest),
        )

    root, inverse = lax.fori_loop(0, NS_STEPS, newton_step, (start_root, start_inverse))
    scale_root = jnp.sqrt(scale)
    orthonormal = jnp.einsum("mrk,mkl->mrl", stacked, inverse, precision=highest) / scale_root
    return (orthonormal, root * scale_root)


def body(samples, sketch, leaf_slot):
    columns = sketch.shape[1]
    leaf_count = leaf_slot.shape[1]
    partial_value = jnp.dot(samples, sketch, precision=highest).reshape(leaf_count, -1, columns)
    sketched = lax.psum(partial_value, "samp")
    leaf_basis, triangle = factor(sketched)
    factors = triangle[leaf_slot[0]]
    local_list = []
    while factors.shape[0] > 1:
        stacked = factors.reshape(-1, 2 * columns, columns)
        transfer, factors = factor(stacked)
        local_list.append(transfer)
    local_transfer = jnp.concatenate(local_list, axis=0)
    position = lax.axis_index("clus")
    tree_depth = lax.axis_size("clus").bit_length() - 1
    top_out = jnp.zeros((1, 2 * columns, columns), jnp.float32)
    for level_bit in range(tree_depth):
        partner = from_partner(factors, "clus", level_bit)
        upper_half = position >> level_bit & 1 == 1
        stacked = jnp.where(
            upper_half,
            jnp.concatenate([partner, factors], axis=1),
            jnp.concatenate([factors, partner], axis=1),
        )
        transfer, factors = factor(stacked)
        owned = position % (2 << level_bit) == 1 << level_bit
        top_out = jnp.where(owned, transfer, top_out)
    return (leaf_basis.reshape(-1, columns), local_transfer, top_out, factors[0])


def solution(mesh):
    return jax.shard_map(
        body,
        mesh=mesh,
        in_specs=(P("clus", "samp"), P("samp", None), P("clus", None)),
        out_specs=(P("clus", None), P("clus", None, None), P("clus", None, None), P()),
        check_vma=False,
    )
```

profile of v0, /device:TPU:32, one launch (start us, length us, event | category | flops | bytes accessed | tf_op | source)
XLA Modules:
  0.0 200.3 jit_solution(17816542363103940892)
XLA Ops:
  7.2 1.0 copy-done
  8.2 2.2 %fusion.137 = f32[1024,128]{1,0:T(8,128)} fusion(f32[1024,128]{1,0:T(8,128)S(1)} %copy-done, f32[128,128]{1,0:T(8,128)} %param.26), kind=kOutput, calls=%fused_computation.230 | convolution fusion | flops 201326592 | bytes 1114112 | tf_op jit(solution)/shard_map/dot_general | solution.py:45
  11.1 0.7 copy-done.12
  11.8 39.1 %all-reduce.2.cloned.1.call-done = f32[4,256,128]{2,1,0:T(8,128)} async-done(((f32[4,256,128]{2,1,0:T(8,128)}), f32[4,256,128]{2,1,0:T(8,128)}) %all-reduce.2.cloned.1.call-update) | async-done | bytes 524304 | tf_op jit(solution)/shard_map/psum | solution.py:46
  50.9 2.3 %select_reduce_fusion = (f32[4]{0:T(128)S(1)}, f32[4,128,128]{2,1,0:T(8,128)S(1)}) fusion(pred[128,128]{1,0:T(8,128)(4,1)S(1)} %iota_compare_fusion.13, f32[4,256,128]{2,1,0:T(8,128)} %all-reduce.2.cloned.1.call-done), kind=kOutput, calls=%fused_computation.126 | convolution fusion | flops 201457664 | bytes 802832 | tf_op jit(solution)/shard_map/mrk,mrl->mkl/dot_general | solution.py:21
  53.5 8.8 %while.143 = (s32[]{:T(128)}, f32[4,128,128]{1,2,0:T(8,128)S(1)}, f32[4,128,128]{2,1,0:T(8,128)S(1)}, s32[]{:T(128)}) while((s32[]{:T(128)}, f32[4,128,128]{1,2,0:T(8,128)S(1)}, f32[4,128,128]{2,1,0:T(8,128)S(1)}, s32[]{:T(128)}) %tuple.231), condition=%wide.region_3.0_spmd.clone, body=%wide.region_2.0_spmd.clone.sunk | while | flops 302153728 | bytes 3538997 | solution.py:36
  53.6 0.7 fusion.277
  54.3 0.6 convolution_bitcast_fusion.41
  55.4 0.7 fusion.277
  56.0 0.6 convolution_bitcast_fusion.41
  57.1 0.7 fusion.277
  57.8 0.6 convolution_bitcast_fusion.41
  58.9 0.7 fusion.277
  59.6 0.6 convolution_bitcast_fusion.41
  60.7 0.7 fusion.277
  61.3 0.6 convolution_bitcast_fusion.41
  63.2 0.7 select_reduce_fusion.1
  64.1 5.6 %while.144 = (s32[]{:T(128)}, f32[2,128,128]{1,2,0:T(8,128)S(1)}, f32[2,128,128]{2,1,0:T(8,128)S(1)}, s32[]{:T(128)}) while((s32[]{:T(128)}, f32[2,128,128]{1,2,0:T(8,128)S(1)}, f32[2,128,128]{2,1,0:T(8,128)S(1)}, s32[]{:T(128)}) %tuple.234), condition=%wide.region_6.0_spmd.clone, body=%wide.region_5.0_spmd.clone.sunk | while | flops 151093248 | bytes 1835061 | solution.py:36
  69.9 1.0 select_reduce_fusion.10
  71.7 0.7 copy-done.3
  72.5 4.1 %while.145 = (s32[]{:T(128)}, f32[1,128,128]{1,2,0:T(8,128)S(1)}, f32[1,128,128]{2,1,0:T(8,128)S(1)}, s32[]{:T(128)}) while((s32[]{:T(128)}, f32[1,128,128]{1,2,0:T(8,128)S(1)}, f32[1,128,128]{2,1,0:T(8,128)S(1)}, s32[]{:T(128)}) %tuple.267), condition=%wide.region_9.0_spmd.clone, body=%wide.region_8.0_spmd.clone.sunk | while | flops 75563008 | bytes 852021 | solution.py:36
  76.9 3.4 %collective-permute-start = (f32[1,128,128]{1,2,0:T(8,128)S(1)}, f32[1,128,128]{1,2,0:T(8,128)S(1)}, u32[]{:S(2)}, u32[]{:S(2)}) collective-permute-start(f32[1,128,128]{1,2,0:T(8,128)S(1)} %broadcast_multiply_fusion.9), channel_id=1, source_target_pairs={{0,2},{2,0},{4,6},{6,4},{8,10},{10,8},{12,14},{14,12},{16,18},{18,... | collective-permute-start | bytes 196616 | tf_op jit(solution)/shard_map/ppermute | solution.py:17
  80.6 1.4 convolution_divide_fusion
  82.0 0.8 pad_maximum_fusion
  83.1 0.9 select_reduce_fusion.9
  84.8 0.7 copy-done.4
  85.6 4.1 %while.146 = (s32[]{:T(128)}, f32[1,128,128]{1,2,0:T(8,128)S(1)}, f32[1,128,128]{2,1,0:T(8,128)S(1)}, s32[]{:T(128)}) while((s32[]{:T(128)}, f32[1,128,128]{1,2,0:T(8,128)S(1)}, f32[1,128,128]{2,1,0:T(8,128)S(1)}, s32[]{:T(128)}) %tuple.268), condition=%wide.region_12.13_spmd.clone, body=%wide.region_11.12_spmd.clone.sunk | while | flops 75563008 | bytes 852021 | solution.py:36
  89.6 4.9 %collective-permute-start.1 = (f32[1,128,128]{1,2,0:T(8,128)S(1)}, f32[1,128,128]{1,2,0:T(8,128)S(1)}, u32[]{:S(2)}, u32[]{:S(2)}) collective-permute-start(f32[1,128,128]{1,2,0:T(8,128)S(1)} %broadcast_multiply_fusion.8), channel_id=1, source_target_pairs={{0,4},{4,0},{2,6},{6,2},{8,12},{12,8},{10,14},{14,10},{16,20},{20,... | collective-permute-start | bytes 196616 | tf_op jit(solution)/shard_map/ppermute | solution.py:17
  95.0 2.4 %collective-permute-done.1 = f32[1,128,128]{1,2,0:T(8,128)S(1)} collective-permute-done((f32[1,128,128]{1,2,0:T(8,128)S(1)}, f32[1,128,128]{1,2,0:T(8,128)S(1)}, u32[]{:S(2)}, u32[]{:S(2)}) %collective-permute-start.1) | collective-permute-done | bytes 65568 | tf_op jit(solution)/shard_map/ppermute | solution.py:17
  97.3 0.9 select_reduce_fusion.8
  99.0 0.7 copy-done.5
  99.7 4.1 %while.147 = (s32[]{:T(128)}, f32[1,128,128]{1,2,0:T(8,128)S(1)}, f32[1,128,128]{2,1,0:T(8,128)S(1)}, s32[]{:T(128)}) while((s32[]{:T(128)}, f32[1,128,128]{1,2,0:T(8,128)S(1)}, f32[1,128,128]{2,1,0:T(8,128)S(1)}, s32[]{:T(128)}) %tuple.269), condition=%wide.region_15.16_spmd.clone, body=%wide.region_14.15_spmd.clone.sunk | while | flops 75563008 | bytes 852021 | solution.py:36
  103.8 2.5 %collective-permute-start.2 = (f32[1,128,128]{1,2,0:T(8,128)S(1)}, f32[1,128,128]{1,2,0:T(8,128)S(1)}, u32[]{:S(2)}, u32[]{:S(2)}) collective-permute-start(f32[1,128,128]{1,2,0:T(8,128)S(1)} %broadcast_multiply_fusion.7), channel_id=1, source_target_pairs={{0,8},{8,0},{2,10},{10,2},{4,12},{12,4},{6,14},{14,6},{16,24},{24,... | collective-permute-start | bytes 196616 | tf_op jit(solution)/shard_map/ppermute | solution.py:17
  106.7 3.2 %collective-permute-done.2 = f32[1,128,128]{1,2,0:T(8,128)S(1)} collective-permute-done((f32[1,128,128]{1,2,0:T(8,128)S(1)}, f32[1,128,128]{1,2,0:T(8,128)S(1)}, u32[]{:S(2)}, u32[]{:S(2)}) %collective-permute-start.2) | collective-permute-done | bytes 65568 | tf_op jit(solution)/shard_map/ppermute | solution.py:17
  110.0 0.9 select_reduce_fusion.7
  111.7 0.7 copy-done.6
  112.4 4.1 %while.148 = (s32[]{:T(128)}, f32[1,128,128]{1,2,0:T(8,128)S(1)}, f32[1,128,128]{2,1,0:T(8,128)S(1)}, s32[]{:T(128)}) while((s32[]{:T(128)}, f32[1,128,128]{1,2,0:T(8,128)S(1)}, f32[1,128,128]{2,1,0:T(8,128)S(1)}, s32[]{:T(128)}) %tuple.270), condition=%wide.region_18.19_spmd.clone, body=%wide.region_17.18_spmd.clone.sunk | while | flops 75563008 | bytes 852021 | solution.py:36
  116.5 2.5 %collective-permute-start.3 = (f32[1,128,128]{1,2,0:T(8,128)S(1)}, f32[1,128,128]{1,2,0:T(8,128)S(1)}, u32[]{:S(2)}, u32[]{:S(2)}) collective-permute-start(f32[1,128,128]{1,2,0:T(8,128)S(1)} %broadcast_multiply_fusion.6), channel_id=1, source_target_pairs={{0,16},{16,0},{2,18},{18,2},{4,20},{20,4},{6,22},{22,6},{8,24},{24... | collective-permute-start | bytes 196616 | tf_op jit(solution)/shard_map/ppermute | solution.py:17
  119.4 4.8 %collective-permute-done.3 = f32[1,128,128]{1,2,0:T(8,128)S(1)} collective-permute-done((f32[1,128,128]{1,2,0:T(8,128)S(1)}, f32[1,128,128]{1,2,0:T(8,128)S(1)}, u32[]{:S(2)}, u32[]{:S(2)}) %collective-permute-start.3) | collective-permute-done | bytes 65568 | tf_op jit(solution)/shard_map/ppermute | solution.py:17
  124.3 0.9 select_reduce_fusion.6
  126.0 0.7 copy-done.7
  126.7 4.1 %while.149 = (s32[]{:T(128)}, f32[1,128,128]{1,2,0:T(8,128)S(1)}, f32[1,128,128]{2,1,0:T(8,128)S(1)}, s32[]{:T(128)}) while((s32[]{:T(128)}, f32[1,128,128]{1,2,0:T(8,128)S(1)}, f32[1,128,128]{2,1,0:T(8,128)S(1)}, s32[]{:T(128)}) %tuple.271), condition=%wide.region_21.22_spmd.clone, body=%wide.region_20.21_spmd.clone.sunk | while | flops 75563008 | bytes 852021 | solution.py:36
  130.8 3.5 %collective-permute-start.4 = (f32[1,128,128]{1,2,0:T(8,128)S(1)}, f32[1,128,128]{1,2,0:T(8,128)S(1)}, u32[]{:S(2)}, u32[]{:S(2)}) collective-permute-start(f32[1,128,128]{1,2,0:T(8,128)S(1)} %broadcast_multiply_fusion.5), channel_id=1, source_target_pairs={{0,32},{32,0},{2,34},{34,2},{4,36},{36,4},{6,38},{38,6},{8,40},{40... | collective-permute-start | bytes 196616 | tf_op jit(solution)/shard_map/ppermute | solution.py:17
  134.7 6.2 %collective-permute-done.4 = f32[1,128,128]{1,2,0:T(8,128)S(1)} collective-permute-done((f32[1,128,128]{1,2,0:T(8,128)S(1)}, f32[1,128,128]{1,2,0:T(8,128)S(1)}, u32[]{:S(2)}, u32[]{:S(2)}) %collective-permute-start.4) | collective-permute-done | bytes 65568 | tf_op jit(solution)/shard_map/ppermute | solution.py:17
  140.9 0.9 select_reduce_fusion.5
  142.6 0.7 copy-done.8
  143.3 4.1 %while.150 = (s32[]{:T(128)}, f32[1,128,128]{1,2,0:T(8,128)S(1)}, f32[1,128,128]{2,1,0:T(8,128)S(1)}, s32[]{:T(128)}) while((s32[]{:T(128)}, f32[1,128,128]{1,2,0:T(8,128)S(1)}, f32[1,128,128]{2,1,0:T(8,128)S(1)}, s32[]{:T(128)}) %tuple.272), condition=%wide.region_24.25_spmd.clone, body=%wide.region_23.24_spmd.clone.sunk | while | flops 75563008 | bytes 852021 | solution.py:36
  147.4 4.0 %collective-permute-start.5 = (f32[1,128,128]{1,2,0:T(8,128)S(1)}, f32[1,128,128]{1,2,0:T(8,128)S(1)}, u32[]{:S(2)}, u32[]{:S(2)}) collective-permute-start(f32[1,128,128]{1,2,0:T(8,128)S(1)} %broadcast_multiply_fusion.4), channel_id=1, source_target_pairs={{0,64},{64,0},{2,66},{66,2},{4,68},{68,4},{6,70},{70,6},{8,72},{72... | collective-permute-start | bytes 196616 | tf_op jit(solution)/shard_map/ppermute | solution.py:17
  151.8 1.8 collective-permute-done.5
  153.6 0.9 select_reduce_fusion.4
  155.3 0.7 copy-done.9
  156.1 4.1 %while.151 = (s32[]{:T(128)}, f32[1,128,128]{1,2,0:T(8,128)S(1)}, f32[1,128,128]{2,1,0:T(8,128)S(1)}, s32[]{:T(128)}) while((s32[]{:T(128)}, f32[1,128,128]{1,2,0:T(8,128)S(1)}, f32[1,128,128]{2,1,0:T(8,128)S(1)}, s32[]{:T(128)}) %tuple.273), condition=%wide.region_27.28_spmd.clone, body=%wide.region_26.27_spmd.clone.sunk | while | flops 75563008 | bytes 852021 | solution.py:36
  160.2 5.0 %collective-permute-start.6 = (f32[1,128,128]{1,2,0:T(8,128)S(1)}, f32[1,128,128]{1,2,0:T(8,128)S(1)}, u32[]{:S(2)}, u32[]{:S(2)}) collective-permute-start(f32[1,128,128]{1,2,0:T(8,128)S(1)} %broadcast_multiply_fusion.3), channel_id=1, source_target_pairs={{0,128},{128,0},{2,130},{130,2},{4,132},{132,4},{6,134},{134,6},{8... | collective-permute-start | bytes 196616 | tf_op jit(solution)/shard_map/ppermute | solution.py:17
  165.6 1.8 collective-permute-done.6
  167.4 0.9 select_reduce_fusion.3
  169.1 0.7 copy-done.10
  169.8 4.1 %while.152 = (s32[]{:T(128)}, f32[1,128,128]{1,2,0:T(8,128)S(1)}, f32[1,128,128]{2,1,0:T(8,128)S(1)}, s32[]{:T(128)}) while((s32[]{:T(128)}, f32[1,128,128]{1,2,0:T(8,128)S(1)}, f32[1,128,128]{2,1,0:T(8,128)S(1)}, s32[]{:T(128)}) %tuple.274), condition=%wide.region_30.31_spmd.clone, body=%wide.region_29.30_spmd.clone.sunk | while | flops 75563008 | bytes 852021 | solution.py:36
  173.9 8.9 %collective-permute-start.7 = (f32[1,128,128]{1,2,0:T(8,128)S(1)}, f32[1,128,128]{1,2,0:T(8,128)S(1)}, u32[]{:S(2)}, u32[]{:S(2)}) collective-permute-start(f32[1,128,128]{1,2,0:T(8,128)S(1)} %broadcast_multiply_fusion.2), channel_id=1, source_target_pairs={{0,256},{256,0},{2,258},{258,2},{4,260},{260,4},{6,262},{262,6},{8... | collective-permute-start | bytes 196616 | tf_op jit(solution)/shard_map/ppermute | solution.py:17
  183.2 1.9 collective-permute-done.7
  185.2 0.9 select_reduce_fusion.2
  186.9 0.7 copy-done.2
  187.6 4.1 %while.153 = (s32[]{:T(128)}, f32[1,128,128]{1,2,0:T(8,128)S(1)}, f32[1,128,128]{2,1,0:T(8,128)S(1)}, s32[]{:T(128)}) while((s32[]{:T(128)}, f32[1,128,128]{1,2,0:T(8,128)S(1)}, f32[1,128,128]{2,1,0:T(8,128)S(1)}, s32[]{:T(128)}) %tuple.266), condition=%wide.region_33.34_spmd.clone, body=%wide.region_32.33_spmd.clone.sunk | while | flops 75563008 | bytes 852021 | solution.py:36
  191.8 0.6 multiply_bitcast_fusion
  192.4 1.0 fusion.73
  (355 shorter events, 49.2 us)
Async XLA Ops:
  7.2 1.0 copy-start
  7.2 43.8 %all-reduce.2.cloned.1.call-start = ((), (), s32[]{:S(2)}) async-start(), calls=%async_computation | async-start | bytes 1048576 | tf_op jit(solution)/shard_map/psum | solution.py:46
  10.5 0.6 copy-start.1
  11.1 0.7 copy-start.12
  71.6 0.8 copy-start.3
  76.6 4.0 %copy-start.11 = (f32[4,256,128]{2,1,0:T(8,128)S(1)}, f32[4,256,128]{2,1,0:T(8,128)}, u32[]{:S(2)}) copy-start(f32[4,256,128]{2,1,0:T(8,128)} %all-reduce.2.cloned.1.call-done) | copy-start | bytes 1572868
  76.9 6.2 %collective-permute-start = (f32[1,128,128]{1,2,0:T(8,128)S(1)}, f32[1,128,128]{1,2,0:T(8,128)S(1)}, u32[]{:S(2)}, u32[]{:S(2)}) collective-permute-start(f32[1,128,128]{1,2,0:T(8,128)S(1)} %broadcast_multiply_fusion.9), channel_id=1, source_target_pairs={{0,2},{2,0},{4,6},{6,4},{8,10},{10,8},{12,14},{14,12},{16,18},{18,... | collective-permute-start | bytes 196616 | tf_op jit(solution)/shard_map/ppermute | solution.py:17
  84.7 0.8 copy-start.4
  89.6 7.7 %collective-permute-start.1 = (f32[1,128,128]{1,2,0:T(8,128)S(1)}, f32[1,128,128]{1,2,0:T(8,128)S(1)}, u32[]{:S(2)}, u32[]{:S(2)}) collective-permute-start(f32[1,128,128]{1,2,0:T(8,128)S(1)} %broadcast_multiply_fusion.8), channel_id=1, source_target_pairs={{0,4},{4,0},{2,6},{6,2},{8,12},{12,8},{10,14},{14,10},{16,20},{20,... | collective-permute-start | bytes 196616 | tf_op jit(solution)/shard_map/ppermute | solution.py:17
  98.9 0.8 copy-start.5
  103.8 6.2 %collective-permute-start.2 = (f32[1,128,128]{1,2,0:T(8,128)S(1)}, f32[1,128,128]{1,2,0:T(8,128)S(1)}, u32[]{:S(2)}, u32[]{:S(2)}) collective-permute-start(f32[1,128,128]{1,2,0:T(8,128)S(1)} %broadcast_multiply_fusion.7), channel_id=1, source_target_pairs={{0,8},{8,0},{2,10},{10,2},{4,12},{12,4},{6,14},{14,6},{16,24},{24,... | collective-permute-start | bytes 196616 | tf_op jit(solution)/shard_map/ppermute | solution.py:17
  111.6 0.8 copy-start.6
  116.5 7.8 %collective-permute-start.3 = (f32[1,128,128]{1,2,0:T(8,128)S(1)}, f32[1,128,128]{1,2,0:T(8,128)S(1)}, u32[]{:S(2)}, u32[]{:S(2)}) collective-permute-start(f32[1,128,128]{1,2,0:T(8,128)S(1)} %broadcast_multiply_fusion.6), channel_id=1, source_target_pairs={{0,16},{16,0},{2,18},{18,2},{4,20},{20,4},{6,22},{22,6},{8,24},{24... | collective-permute-start | bytes 196616 | tf_op jit(solution)/shard_map/ppermute | solution.py:17
  125.9 0.8 copy-start.7
  130.8 10.1 %collective-permute-start.4 = (f32[1,128,128]{1,2,0:T(8,128)S(1)}, f32[1,128,128]{1,2,0:T(8,128)S(1)}, u32[]{:S(2)}, u32[]{:S(2)}) collective-permute-start(f32[1,128,128]{1,2,0:T(8,128)S(1)} %broadcast_multiply_fusion.5), channel_id=1, source_target_pairs={{0,32},{32,0},{2,34},{34,2},{4,36},{36,4},{6,38},{38,6},{8,40},{40... | collective-permute-start | bytes 196616 | tf_op jit(solution)/shard_map/ppermute | solution.py:17
  142.5 0.8 copy-start.8
  147.4 6.2 %collective-permute-start.5 = (f32[1,128,128]{1,2,0:T(8,128)S(1)}, f32[1,128,128]{1,2,0:T(8,128)S(1)}, u32[]{:S(2)}, u32[]{:S(2)}) collective-permute-start(f32[1,128,128]{1,2,0:T(8,128)S(1)} %broadcast_multiply_fusion.4), channel_id=1, source_target_pairs={{0,64},{64,0},{2,66},{66,2},{4,68},{68,4},{6,70},{70,6},{8,72},{72... | collective-permute-start | bytes 196616 | tf_op jit(solution)/shard_map/ppermute | solution.py:17
  155.2 0.8 copy-start.9
  160.2 7.2 %collective-permute-start.6 = (f32[1,128,128]{1,2,0:T(8,128)S(1)}, f32[1,128,128]{1,2,0:T(8,128)S(1)}, u32[]{:S(2)}, u32[]{:S(2)}) collective-permute-start(f32[1,128,128]{1,2,0:T(8,128)S(1)} %broadcast_multiply_fusion.3), channel_id=1, source_target_pairs={{0,128},{128,0},{2,130},{130,2},{4,132},{132,4},{6,134},{134,6},{8... | collective-permute-start | bytes 196616 | tf_op jit(solution)/shard_map/ppermute | solution.py:17
  169.0 0.8 copy-start.10
  173.9 11.2 %collective-permute-start.7 = (f32[1,128,128]{1,2,0:T(8,128)S(1)}, f32[1,128,128]{1,2,0:T(8,128)S(1)}, u32[]{:S(2)}, u32[]{:S(2)}) collective-permute-start(f32[1,128,128]{1,2,0:T(8,128)S(1)} %broadcast_multiply_fusion.2), channel_id=1, source_target_pairs={{0,256},{256,0},{2,258},{258,2},{4,260},{260,4},{6,262},{262,6},{8... | collective-permute-start | bytes 196616 | tf_op jit(solution)/shard_map/ppermute | solution.py:17
  186.7 0.8 copy-start.2
Sparse Core Ops, SparseCore 0:
  11.5 39.4 all-reduce.1
where the time goes:
time: 201 us; the launch traced here: 200 us
  matrix products  66.6 us (33%)
  waiting for transfers between devices  61.6 us (31%)
  starting transfers between devices  34.7 us (17%)
  between operations  21 us (10%)
  local copies, waits for them, and re-layouts  11.7 us (6%)
  loops' own time  2.47 us (1%)
  other arithmetic  2.16 us (1%)
    psum x1, waiting for transfers between devices, body(): sketched = lax.psum(partial_value, 'samp')  39.1 us
    ppermute x8, starting transfers between devices, from_partner(): return lax.ppermute(block, axis, route)  34.7 us
    ppermute x8, waiting for transfers between devices, from_partner(): return lax.ppermute(block, axis, route)  22.5 us
    dot_general x55, matrix products, newton_step(): jnp.einsum('mkl,mlj->mkj', root, middle, precision=highest)  17.8 us
    dot_general x55, matrix products, newton_step(): jnp.einsum('mkl,mlj->mkj', inverse, root, precision=highest)  17.3 us
    dot_general x55, matrix products, newton_step(): jnp.einsum('mkl,mlj->mkj', middle, inverse, precision=highest)  12.4 us
    dot_general x11, matrix products, factor(): jnp.einsum('mrk,mrl->mkl', stacked, stacked, precision=highest)  11 us
    unnamed x37, local copies, waits for them, and re-layouts  9.91 us
  transfers between devices with their start and end apart: 9, of which 9 were waited for; matrix products, arithmetic and copies ran while one was open for 3% of the time, Pallas kernels for 0%

commit v1 on v0

--- a/solution.py
+++ b/solution.py
@@ -43,7 +43,7 @@
     columns = sketch.shape[1]
     leaf_count = leaf_slot.shape[1]
     partial_value = jnp.dot(samples, sketch, precision=highest).reshape(leaf_count, -1, columns)
-    sketched = lax.psum(partial_value, "samp")
+    sketched = jnp.sum(lax.all_gather(partial_value, "samp"), axis=0)
     leaf_basis, triangle = factor(sketched)
     factors = triangle[leaf_slot[0]]
     local_list = []

time: 201 us -> 184 us (0.915)
  waiting for transfers between devices: 61.6 us -> 44.3 us
    psum x1 -> x0, waiting for transfers between devices: 39.1 us -> none  [body(): sketched = lax.psum(partial_value, 'samp')]
    all_gather x0 -> x1, waiting for transfers between devices: none -> 20.4 us  [body(): sketched = jnp.sum(lax.all_gather(partial_value, 'samp'), axis=0)]
    unnamed x37 -> x35, local copies, waits for them, and re-layouts: 9.91 us -> 9.91 us
  transfers between devices with their start and end apart: 9 -> 9, of which waited for: 9 -> 9; matrix products, arithmetic and copies ran while one was open for 3% -> 2% of each run, Pallas kernels for 0% -> 0%
where the time goes in v1:
time: 184 us; the launch traced here: 183 us
  matrix products  65.4 us (36%)
  waiting for transfers between devices  44.3 us (24%)
  starting transfers between devices  34.7 us (19%)
  between operations  21 us (11%)
  local copies, waits for them, and re-layouts  11.7 us (6%)
  other arithmetic  3.51 us (2%)
  loops' own time  2.47 us (1%)
    ppermute x8, starting transfers between devices, from_partner(): return lax.ppermute(block, axis, route)  34.7 us
    ppermute x8, waiting for transfers between devices, from_partner(): return lax.ppermute(block, axis, route)  23.9 us
    all_gather x1, waiting for transfers between devices, body(): sketched = jnp.sum(lax.all_gather(partial_value, 'samp'), axis=0)  20.4 us
    dot_general x55, matrix products, newton_step(): jnp.einsum('mkl,mlj->mkj', root, middle, precision=highest)  17.8 us
    dot_general x55, matrix products, newton_step(): jnp.einsum('mkl,mlj->mkj', inverse, root, precision=highest)  17.3 us
    dot_general x55, matrix products, newton_step(): jnp.einsum('mkl,mlj->mkj', middle, inverse, precision=highest)  12.4 us
    unnamed x35, local copies, waits for them, and re-layouts  9.91 us
    dot_general x11, matrix products, factor(): jnp.einsum('mrk,mrl->mkl', stacked, stacked, precision=highest)  9.8 us
  transfers between devices with their start and end apart: 9, of which 9 were waited for; matrix products, arithmetic and copies ran while one was open for 2% of the time, Pallas kernels for 0%

profile of v1, /device:TPU:32, one launch (start us, length us, event | category | flops | bytes accessed | tf_op | source)
XLA Modules:
  0.0 183.1 jit_solution(2888992823658169233)
XLA Ops:
  7.2 1.0 copy-done
  8.2 2.2 %fusion.137 = f32[1024,128]{1,0:T(8,128)} fusion(f32[1024,128]{1,0:T(8,128)S(1)} %copy-done, f32[128,128]{1,0:T(8,128)} %param.26), kind=kOutput, calls=%fused_computation.230 | convolution fusion | flops 201326592 | bytes 1114112 | tf_op jit(solution)/shard_map/dot_general | solution.py:45
  11.1 0.7 copy-done.11
  11.8 20.4 %all-gather.2.cloned.1.call-done = f32[2,4,256,128]{3,2,1,0:T(8,128)} async-done(((f32[1,4,256,128]{3,2,1,0:T(8,128)}), f32[2,4,256,128]{3,2,1,0:T(8,128)}) %all-gather.2.cloned.1.call-update) | async-done | bytes 1048592 | tf_op jit(solution)/shard_map/all_gather | solution.py:46
  32.2 1.3 reduce_sum.108
  33.5 1.1 select_reduce_fusion
  34.9 8.8 %while.143 = (s32[]{:T(128)}, f32[4,128,128]{1,2,0:T(8,128)S(1)}, f32[4,128,128]{2,1,0:T(8,128)S(1)}, s32[]{:T(128)}) while((s32[]{:T(128)}, f32[4,128,128]{1,2,0:T(8,128)S(1)}, f32[4,128,128]{2,1,0:T(8,128)S(1)}, s32[]{:T(128)}) %tuple.242), condition=%wide.region_3.0_spmd.clone, body=%wide.region_2.0_spmd.clone.sunk | while | flops 302153728 | bytes 3538997 | solution.py:36
  35.0 0.7 fusion.277
  35.6 0.6 convolution_bitcast_fusion.41
  36.7 0.7 fusion.277
  37.4 0.6 convolution_bitcast_fusion.41
  38.5 0.7 fusion.277
  39.2 0.6 convolution_bitcast_fusion.41
  40.3 0.7 fusion.277
  42.1 0.7 fusion.277
  44.5 0.7 select_reduce_fusion.1
  45.5 5.6 %while.144 = (s32[]{:T(128)}, f32[2,128,128]{1,2,0:T(8,128)S(1)}, f32[2,128,128]{2,1,0:T(8,128)S(1)}, s32[]{:T(128)}) while((s32[]{:T(128)}, f32[2,128,128]{1,2,0:T(8,128)S(1)}, f32[2,128,128]{2,1,0:T(8,128)S(1)}, s32[]{:T(128)}) %tuple.245), condition=%wide.region_6.0_spmd.clone, body=%wide.region_5.0_spmd.clone.sunk | while | flops 151093248 | bytes 1835061 | solution.py:36
  51.3 1.0 select_reduce_fusion.10
  53.1 0.7 copy-done.3
  53.8 4.1 %while.145 = (s32[]{:T(128)}, f32[1,128,128]{1,2,0:T(8,128)S(1)}, f32[1,128,128]{2,1,0:T(8,128)S(1)}, s32[]{:T(128)}) while((s32[]{:T(128)}, f32[1,128,128]{1,2,0:T(8,128)S(1)}, f32[1,128,128]{2,1,0:T(8,128)S(1)}, s32[]{:T(128)}) %tuple.278), condition=%wide.region_9.0_spmd.clone, body=%wide.region_8.0_spmd.clone.sunk | while | flops 75563008 | bytes 852021 | solution.py:36
  57.9 1.4 convolution_divide_fusion
  59.7 3.4 %collective-permute-start = (f32[1,128,128]{1,2,0:T(8,128)S(1)}, f32[1,128,128]{1,2,0:T(8,128)S(1)}, u32[]{:S(2)}, u32[]{:S(2)}) collective-permute-start(f32[1,128,128]{1,2,0:T(8,128)S(1)} %broadcast_multiply_fusion.9), channel_id=1, source_target_pairs={{0,2},{2,0},{4,6},{6,4},{8,10},{10,8},{12,14},{14,12},{16,18},{18,... | collective-permute-start | bytes 196616 | tf_op jit(solution)/shard_map/ppermute | solution.py:17
  63.4 0.8 pad_maximum_fusion
  64.1 1.8 collective-permute-done
  65.9 0.9 select_reduce_fusion.9
  67.6 0.7 copy-done.4
  68.3 4.1 %while.146 = (s32[]{:T(128)}, f32[1,128,128]{1,2,0:T(8,128)S(1)}, f32[1,128,128]{2,1,0:T(8,128)S(1)}, s32[]{:T(128)}) while((s32[]{:T(128)}, f32[1,128,128]{1,2,0:T(8,128)S(1)}, f32[1,128,128]{2,1,0:T(8,128)S(1)}, s32[]{:T(128)}) %tuple.279), condition=%wide.region_12.13_spmd.clone, body=%wide.region_11.12_spmd.clone.sunk | while | flops 75563008 | bytes 852021 | solution.py:36
  72.4 4.9 %collective-permute-start.1 = (f32[1,128,128]{1,2,0:T(8,128)S(1)}, f32[1,128,128]{1,2,0:T(8,128)S(1)}, u32[]{:S(2)}, u32[]{:S(2)}) collective-permute-start(f32[1,128,128]{1,2,0:T(8,128)S(1)} %broadcast_multiply_fusion.8), channel_id=1, source_target_pairs={{0,4},{4,0},{2,6},{6,2},{8,12},{12,8},{10,14},{14,10},{16,20},{20,... | collective-permute-start | bytes 196616 | tf_op jit(solution)/shard_map/ppermute | solution.py:17
  77.7 2.4 %collective-permute-done.1 = f32[1,128,128]{1,2,0:T(8,128)S(1)} collective-permute-done((f32[1,128,128]{1,2,0:T(8,128)S(1)}, f32[1,128,128]{1,2,0:T(8,128)S(1)}, u32[]{:S(2)}, u32[]{:S(2)}) %collective-permute-start.1) | collective-permute-done | bytes 65568 | tf_op jit(solution)/shard_map/ppermute | solution.py:17
  80.1 0.9 select_reduce_fusion.8
  81.8 0.7 copy-done.5
  82.5 4.1 %while.147 = (s32[]{:T(128)}, f32[1,128,128]{1,2,0:T(8,128)S(1)}, f32[1,128,128]{2,1,0:T(8,128)S(1)}, s32[]{:T(128)}) while((s32[]{:T(128)}, f32[1,128,128]{1,2,0:T(8,128)S(1)}, f32[1,128,128]{2,1,0:T(8,128)S(1)}, s32[]{:T(128)}) %tuple.280), condition=%wide.region_15.16_spmd.clone, body=%wide.region_14.15_spmd.clone.sunk | while | flops 75563008 | bytes 852021 | solution.py:36
  86.6 2.5 %collective-permute-start.2 = (f32[1,128,128]{1,2,0:T(8,128)S(1)}, f32[1,128,128]{1,2,0:T(8,128)S(1)}, u32[]{:S(2)}, u32[]{:S(2)}) collective-permute-start(f32[1,128,128]{1,2,0:T(8,128)S(1)} %broadcast_multiply_fusion.7), channel_id=1, source_target_pairs={{0,8},{8,0},{2,10},{10,2},{4,12},{12,4},{6,14},{14,6},{16,24},{24,... | collective-permute-start | bytes 196616 | tf_op jit(solution)/shard_map/ppermute | solution.py:17
  89.5 3.2 %collective-permute-done.2 = f32[1,128,128]{1,2,0:T(8,128)S(1)} collective-permute-done((f32[1,128,128]{1,2,0:T(8,128)S(1)}, f32[1,128,128]{1,2,0:T(8,128)S(1)}, u32[]{:S(2)}, u32[]{:S(2)}) %collective-permute-start.2) | collective-permute-done | bytes 65568 | tf_op jit(solution)/shard_map/ppermute | solution.py:17
  92.8 0.9 select_reduce_fusion.7
  94.5 0.7 copy-done.6
  95.2 4.1 %while.148 = (s32[]{:T(128)}, f32[1,128,128]{1,2,0:T(8,128)S(1)}, f32[1,128,128]{2,1,0:T(8,128)S(1)}, s32[]{:T(128)}) while((s32[]{:T(128)}, f32[1,128,128]{1,2,0:T(8,128)S(1)}, f32[1,128,128]{2,1,0:T(8,128)S(1)}, s32[]{:T(128)}) %tuple.281), condition=%wide.region_18.19_spmd.clone, body=%wide.region_17.18_spmd.clone.sunk | while | flops 75563008 | bytes 852021 | solution.py:36
  99.3 2.5 %collective-permute-start.3 = (f32[1,128,128]{1,2,0:T(8,128)S(1)}, f32[1,128,128]{1,2,0:T(8,128)S(1)}, u32[]{:S(2)}, u32[]{:S(2)}) collective-permute-start(f32[1,128,128]{1,2,0:T(8,128)S(1)} %broadcast_multiply_fusion.6), channel_id=1, source_target_pairs={{0,16},{16,0},{2,18},{18,2},{4,20},{20,4},{6,22},{22,6},{8,24},{24... | collective-permute-start | bytes 196616 | tf_op jit(solution)/shard_map/ppermute | solution.py:17
  102.2 4.8 %collective-permute-done.3 = f32[1,128,128]{1,2,0:T(8,128)S(1)} collective-permute-done((f32[1,128,128]{1,2,0:T(8,128)S(1)}, f32[1,128,128]{1,2,0:T(8,128)S(1)}, u32[]{:S(2)}, u32[]{:S(2)}) %collective-permute-start.3) | collective-permute-done | bytes 65568 | tf_op jit(solution)/shard_map/ppermute | solution.py:17
  107.0 0.9 select_reduce_fusion.6
  108.7 0.7 copy-done.7
  109.5 4.1 %while.149 = (s32[]{:T(128)}, f32[1,128,128]{1,2,0:T(8,128)S(1)}, f32[1,128,128]{2,1,0:T(8,128)S(1)}, s32[]{:T(128)}) while((s32[]{:T(128)}, f32[1,128,128]{1,2,0:T(8,128)S(1)}, f32[1,128,128]{2,1,0:T(8,128)S(1)}, s32[]{:T(128)}) %tuple.282), condition=%wide.region_21.22_spmd.clone, body=%wide.region_20.21_spmd.clone.sunk | while | flops 75563008 | bytes 852021 | solution.py:36
  113.6 3.5 %collective-permute-start.4 = (f32[1,128,128]{1,2,0:T(8,128)S(1)}, f32[1,128,128]{1,2,0:T(8,128)S(1)}, u32[]{:S(2)}, u32[]{:S(2)}) collective-permute-start(f32[1,128,128]{1,2,0:T(8,128)S(1)} %broadcast_multiply_fusion.5), channel_id=1, source_target_pairs={{0,32},{32,0},{2,34},{34,2},{4,36},{36,4},{6,38},{38,6},{8,40},{40... | collective-permute-start | bytes 196616 | tf_op jit(solution)/shard_map/ppermute | solution.py:17
  117.5 6.2 %collective-permute-done.4 = f32[1,128,128]{1,2,0:T(8,128)S(1)} collective-permute-done((f32[1,128,128]{1,2,0:T(8,128)S(1)}, f32[1,128,128]{1,2,0:T(8,128)S(1)}, u32[]{:S(2)}, u32[]{:S(2)}) %collective-permute-start.4) | collective-permute-done | bytes 65568 | tf_op jit(solution)/shard_map/ppermute | solution.py:17
  123.7 0.9 select_reduce_fusion.5
  125.4 0.7 copy-done.8
  126.1 4.1 %while.150 = (s32[]{:T(128)}, f32[1,128,128]{1,2,0:T(8,128)S(1)}, f32[1,128,128]{2,1,0:T(8,128)S(1)}, s32[]{:T(128)}) while((s32[]{:T(128)}, f32[1,128,128]{1,2,0:T(8,128)S(1)}, f32[1,128,128]{2,1,0:T(8,128)S(1)}, s32[]{:T(128)}) %tuple.283), condition=%wide.region_24.25_spmd.clone, body=%wide.region_23.24_spmd.clone.sunk | while | flops 75563008 | bytes 852021 | solution.py:36
  130.2 4.0 %collective-permute-start.5 = (f32[1,128,128]{1,2,0:T(8,128)S(1)}, f32[1,128,128]{1,2,0:T(8,128)S(1)}, u32[]{:S(2)}, u32[]{:S(2)}) collective-permute-start(f32[1,128,128]{1,2,0:T(8,128)S(1)} %broadcast_multiply_fusion.4), channel_id=1, source_target_pairs={{0,64},{64,0},{2,66},{66,2},{4,68},{68,4},{6,70},{70,6},{8,72},{72... | collective-permute-start | bytes 196616 | tf_op jit(solution)/shard_map/ppermute | solution.py:17
  134.6 1.8 collective-permute-done.5
  136.4 0.9 select_reduce_fusion.4
  138.1 0.7 copy-done.9
  138.9 4.1 %while.151 = (s32[]{:T(128)}, f32[1,128,128]{1,2,0:T(8,128)S(1)}, f32[1,128,128]{2,1,0:T(8,128)S(1)}, s32[]{:T(128)}) while((s32[]{:T(128)}, f32[1,128,128]{1,2,0:T(8,128)S(1)}, f32[1,128,128]{2,1,0:T(8,128)S(1)}, s32[]{:T(128)}) %tuple.284), condition=%wide.region_27.28_spmd.clone, body=%wide.region_26.27_spmd.clone.sunk | while | flops 75563008 | bytes 852021 | solution.py:36
  142.9 5.0 %collective-permute-start.6 = (f32[1,128,128]{1,2,0:T(8,128)S(1)}, f32[1,128,128]{1,2,0:T(8,128)S(1)}, u32[]{:S(2)}, u32[]{:S(2)}) collective-permute-start(f32[1,128,128]{1,2,0:T(8,128)S(1)} %broadcast_multiply_fusion.3), channel_id=1, source_target_pairs={{0,128},{128,0},{2,130},{130,2},{4,132},{132,4},{6,134},{134,6},{8... | collective-permute-start | bytes 196616 | tf_op jit(solution)/shard_map/ppermute | solution.py:17
  148.4 1.8 collective-permute-done.6
  150.2 0.9 select_reduce_fusion.3
  151.9 0.7 copy-done.10
  152.6 4.1 %while.152 = (s32[]{:T(128)}, f32[1,128,128]{1,2,0:T(8,128)S(1)}, f32[1,128,128]{2,1,0:T(8,128)S(1)}, s32[]{:T(128)}) while((s32[]{:T(128)}, f32[1,128,128]{1,2,0:T(8,128)S(1)}, f32[1,128,128]{2,1,0:T(8,128)S(1)}, s32[]{:T(128)}) %tuple.285), condition=%wide.region_30.31_spmd.clone, body=%wide.region_29.30_spmd.clone.sunk | while | flops 75563008 | bytes 852021 | solution.py:36
  156.7 8.9 %collective-permute-start.7 = (f32[1,128,128]{1,2,0:T(8,128)S(1)}, f32[1,128,128]{1,2,0:T(8,128)S(1)}, u32[]{:S(2)}, u32[]{:S(2)}) collective-permute-start(f32[1,128,128]{1,2,0:T(8,128)S(1)} %broadcast_multiply_fusion.2), channel_id=1, source_target_pairs={{0,256},{256,0},{2,258},{258,2},{4,260},{260,4},{6,262},{262,6},{8... | collective-permute-start | bytes 196616 | tf_op jit(solution)/shard_map/ppermute | solution.py:17
  166.0 1.9 %collective-permute-done.7 = f32[1,128,128]{1,2,0:T(8,128)S(1)} collective-permute-done((f32[1,128,128]{1,2,0:T(8,128)S(1)}, f32[1,128,128]{1,2,0:T(8,128)S(1)}, u32[]{:S(2)}, u32[]{:S(2)}) %collective-permute-start.7) | collective-permute-done | bytes 65568 | tf_op jit(solution)/shard_map/ppermute | solution.py:17
  167.9 0.9 select_reduce_fusion.2
  169.6 0.7 copy-done.2
  170.4 4.1 %while.153 = (s32[]{:T(128)}, f32[1,128,128]{1,2,0:T(8,128)S(1)}, f32[1,128,128]{2,1,0:T(8,128)S(1)}, s32[]{:T(128)}) while((s32[]{:T(128)}, f32[1,128,128]{1,2,0:T(8,128)S(1)}, f32[1,128,128]{2,1,0:T(8,128)S(1)}, s32[]{:T(128)}) %tuple.277), condition=%wide.region_33.34_spmd.clone, body=%wide.region_32.33_spmd.clone.sunk | while | flops 75563008 | bytes 852021 | solution.py:36
  174.5 0.6 multiply_bitcast_fusion
  175.2 1.0 fusion.73
  (354 shorter events, 50.1 us)
Async XLA Ops:
  7.2 1.0 copy-start
  7.2 25.0 %all-gather.2.cloned.1.call-start = ((), (), s32[]{:S(2)}) async-start(), calls=%async_computation | async-start | bytes 1572864 | tf_op jit(solution)/shard_map/all_gather | solution.py:46
  10.5 0.6 copy-start.1
  11.1 0.7 copy-start.11
  53.0 0.8 copy-start.3
  59.7 6.2 %collective-permute-start = (f32[1,128,128]{1,2,0:T(8,128)S(1)}, f32[1,128,128]{1,2,0:T(8,128)S(1)}, u32[]{:S(2)}, u32[]{:S(2)}) collective-permute-start(f32[1,128,128]{1,2,0:T(8,128)S(1)} %broadcast_multiply_fusion.9), channel_id=1, source_target_pairs={{0,2},{2,0},{4,6},{6,4},{8,10},{10,8},{12,14},{14,12},{16,18},{18,... | collective-permute-start | bytes 196616 | tf_op jit(solution)/shard_map/ppermute | solution.py:17
  67.5 0.8 copy-start.4
  72.4 7.7 %collective-permute-start.1 = (f32[1,128,128]{1,2,0:T(8,128)S(1)}, f32[1,128,128]{1,2,0:T(8,128)S(1)}, u32[]{:S(2)}, u32[]{:S(2)}) collective-permute-start(f32[1,128,128]{1,2,0:T(8,128)S(1)} %broadcast_multiply_fusion.8), channel_id=1, source_target_pairs={{0,4},{4,0},{2,6},{6,2},{8,12},{12,8},{10,14},{14,10},{16,20},{20,... | collective-permute-start | bytes 196616 | tf_op jit(solution)/shard_map/ppermute | solution.py:17
  81.7 0.8 copy-start.5
  86.6 6.2 %collective-permute-start.2 = (f32[1,128,128]{1,2,0:T(8,128)S(1)}, f32[1,128,128]{1,2,0:T(8,128)S(1)}, u32[]{:S(2)}, u32[]{:S(2)}) collective-permute-start(f32[1,128,128]{1,2,0:T(8,128)S(1)} %broadcast_multiply_fusion.7), channel_id=1, source_target_pairs={{0,8},{8,0},{2,10},{10,2},{4,12},{12,4},{6,14},{14,6},{16,24},{24,... | collective-permute-start | bytes 196616 | tf_op jit(solution)/shard_map/ppermute | solution.py:17
  94.4 0.8 copy-start.6
  99.3 7.8 %collective-permute-start.3 = (f32[1,128,128]{1,2,0:T(8,128)S(1)}, f32[1,128,128]{1,2,0:T(8,128)S(1)}, u32[]{:S(2)}, u32[]{:S(2)}) collective-permute-start(f32[1,128,128]{1,2,0:T(8,128)S(1)} %broadcast_multiply_fusion.6), channel_id=1, source_target_pairs={{0,16},{16,0},{2,18},{18,2},{4,20},{20,4},{6,22},{22,6},{8,24},{24... | collective-permute-start | bytes 196616 | tf_op jit(solution)/shard_map/ppermute | solution.py:17
  108.6 0.8 copy-start.7
  113.6 10.1 %collective-permute-start.4 = (f32[1,128,128]{1,2,0:T(8,128)S(1)}, f32[1,128,128]{1,2,0:T(8,128)S(1)}, u32[]{:S(2)}, u32[]{:S(2)}) collective-permute-start(f32[1,128,128]{1,2,0:T(8,128)S(1)} %broadcast_multiply_fusion.5), channel_id=1, source_target_pairs={{0,32},{32,0},{2,34},{34,2},{4,36},{36,4},{6,38},{38,6},{8,40},{40... | collective-permute-start | bytes 196616 | tf_op jit(solution)/shard_map/ppermute | solution.py:17
  125.3 0.8 copy-start.8
  130.2 6.2 %collective-permute-start.5 = (f32[1,128,128]{1,2,0:T(8,128)S(1)}, f32[1,128,128]{1,2,0:T(8,128)S(1)}, u32[]{:S(2)}, u32[]{:S(2)}) collective-permute-start(f32[1,128,128]{1,2,0:T(8,128)S(1)} %broadcast_multiply_fusion.4), channel_id=1, source_target_pairs={{0,64},{64,0},{2,66},{66,2},{4,68},{68,4},{6,70},{70,6},{8,72},{72... | collective-permute-start | bytes 196616 | tf_op jit(solution)/shard_map/ppermute | solution.py:17
  138.0 0.8 copy-start.9
  142.9 7.2 %collective-permute-start.6 = (f32[1,128,128]{1,2,0:T(8,128)S(1)}, f32[1,128,128]{1,2,0:T(8,128)S(1)}, u32[]{:S(2)}, u32[]{:S(2)}) collective-permute-start(f32[1,128,128]{1,2,0:T(8,128)S(1)} %broadcast_multiply_fusion.3), channel_id=1, source_target_pairs={{0,128},{128,0},{2,130},{130,2},{4,132},{132,4},{6,134},{134,6},{8... | collective-permute-start | bytes 196616 | tf_op jit(solution)/shard_map/ppermute | solution.py:17
  151.8 0.8 copy-start.10
  156.7 11.2 %collective-permute-start.7 = (f32[1,128,128]{1,2,0:T(8,128)S(1)}, f32[1,128,128]{1,2,0:T(8,128)S(1)}, u32[]{:S(2)}, u32[]{:S(2)}) collective-permute-start(f32[1,128,128]{1,2,0:T(8,128)S(1)} %broadcast_multiply_fusion.2), channel_id=1, source_target_pairs={{0,256},{256,0},{2,258},{258,2},{4,260},{260,4},{6,262},{262,6},{8... | collective-permute-start | bytes 196616 | tf_op jit(solution)/shard_map/ppermute | solution.py:17
  169.5 0.8 copy-start.2
Sparse Core Ops, SparseCore 0:
  10.7 21.4 all-gather.1
